TPU v7x, 32 devices: a whole 2x2x4 slice. The times are simulated.
32 devices in a mesh: groups: 2 (over y), range: 8 (over z, x), chan: 2 (over core).
Axes of the slice: x: 2, y: 2, z: 4, core: 2. Of those that a mesh axis runs over, the one named last changes fastest.
Arguments:
- echoes: bfloat16 [4, 512, 8, 1024], P('groups', 'chan', None, 'range'), parts along dimension 0, may hold values from -6 to 6
- chirp: float32 [2, 2049], replicated, may hold values from -0.09375 to 0.09375
- gates: int32 [4, 8], P('groups'), parts along dimension 0, may hold values from 0 to 1023, as said below
Outputs:
- compressed: bfloat16 [4, 512, 8, 1024], P('groups', 'chan', None, 'range'), parts along dimension 0
- covariance: float32 [4, 2, 2048, 4096], P('groups', 'chan', 'range'), parts along dimension 0
There are 2 independent parts, one for each index of `groups`. A program takes and returns all parts, laid end to end along the dimension named above; an argument that names none is the same for every part. Nothing has to cross between parts.
Inputs may be any that keep to these rules, and one draw needn't show every extreme that they name: `gates`: the 8 intervals are given in increasing order, do not intersect, lie within the 1024 cells, each holds one cell or more, and their lengths add up to 128. The first interval starts at cell 0, and the last is the single cell 1024 - 1.
All inputs are finite; a program needn't handle non-finite values.
Results may differ from a plain program's by a relative error of at most 0.0035.
Values may be sent and summed in bfloat16 or wider, within the bound.
No kernel may reach another device: no remote copies, remote signals or barrier semaphores. Data moves between devices by JAX's collectives and lax.ppermute only.
A program may use at most 128 MiB of HBM per device.

v0:
```python
from functools import partial
import math
import jax
import jax.numpy as jnp
from jax import lax
from jax.sharding import PartitionSpec as P

TRAIN = 128


def partner_2(value, axis, bit):
    mask = 2**bit
    pairs = [(source, source ^ mask) for source in range(lax.axis_size(axis))]
    return lax.ppermute(value, axis, pairs)


def as_sent(x):

    def short(part):
        return part.astype(jnp.bfloat16) if part.dtype == jnp.float32 else part

    return jax.tree.map(short, x)


def train_cells(gates, count):
    starts = gates[0]
    widths = gates[1]
    ends = jnp.cumsum(widths)
    places = jnp.arange(count, dtype=jnp.int32)
    which = jnp.sum((ends[None, :] <= places[:, None]).astype(jnp.int32), axis=1)
    onehot = jnp.arange(gates.shape[1], dtype=jnp.int32)[None, :] == which[:, None]
    offset = jnp.sum(jnp.where(onehot, (starts - (ends - widths))[None, :], 0), axis=1)
    return offset + places


def angle_tables(radix, nfft, sign):
    steps = jnp.arange(radix, dtype=jnp.int32)
    square = steps[:, None] * steps[None, :]
    small = sign * 2.0 * math.pi * (square % radix).astype(jnp.float32) / radix
    large = sign * 2.0 * math.pi * square.astype(jnp.float32) / nfft
    small_cos = jnp.cos(small)
    small_sin = jnp.sin(small)
    stacked = jnp.stack([small_cos, small_sin])
    block = jnp.concatenate(
        [
            jnp.concatenate([small_cos, small_sin], axis=1),
            jnp.concatenate([-small_sin, small_cos], axis=1),
        ],
        axis=0,
    )
    twiddle = jnp.concatenate([jnp.cos(large), jnp.sin(large)], axis=1)
    return (stacked, block, twiddle)


def merged_times(first, second):
    half = first.shape[-1] // 2
    first_re = first[..., :half]
    first_im = first[..., half:]
    second_re = second[..., :half]
    second_im = second[..., half:]
    return jnp.concatenate(
        [first_re * second_re - first_im * second_im, first_re * second_im + first_im * second_re],
        axis=-1,
    )


def left_section(stacked, values):
    mixed = jnp.einsum("ckn,...nr->...ckr", stacked, values, precision=lax.Precision.HIGHEST)
    half = values.shape[-1] // 2
    real_part = mixed[..., 0, :, :half] - mixed[..., 1, :, half:]
    imag_part = mixed[..., 1, :, :half] + mixed[..., 0, :, half:]
    return jnp.concatenate([real_part, imag_part], axis=-1)


def right_section(values, block):
    return jnp.einsum("...km,mj->...kj", values, block, precision=lax.Precision.HIGHEST)


def forward_dft(values, tables):
    stacked, block, twiddle = tables
    section = left_section(stacked, values)
    section = merged_times(section, twiddle)
    return right_section(section, block)


def inverse_upper(spectrum, tables):
    stacked, block, twiddle = tables
    section = right_section(spectrum, block)
    section = merged_times(section, twiddle)
    half = stacked.shape[1] // 2
    return left_section(stacked[:, half:], section)


def gram(left, right):
    contract = partial(
        lax.dot_general,
        dimension_numbers=(((1,), (1,)), ((), ())),
        preferred_element_type=jnp.float32,
    )
    real_part = contract(left[0], right[0]) + contract(left[1], right[1])
    imag_part = contract(left[1], right[0]) - contract(left[0], right[1])
    return jnp.stack([real_part, imag_part])


def on_device(echoes, chirp, gates):
    chans = echoes.shape[1]
    pulses = echoes.shape[2]
    cells_dev = echoes.shape[3]
    taps = chirp.shape[1]
    newlen = taps - 1
    nfft = 2 * newlen
    radix = math.isqrt(nfft)
    ranks = lax.axis_size("range")
    range_len = cells_dev * ranks
    nseg = (range_len + newlen - 1) // newlen
    forward_tables = angle_tables(radix, nfft, -1.0)
    inverse_tables = angle_tables(radix, nfft, 1.0)
    padded_taps = jnp.pad(chirp, ((0, 0), (0, nfft - taps))).reshape(2, radix, radix)
    response = forward_dft(
        jnp.concatenate([padded_taps[0], padded_taps[1]], axis=-1), forward_tables
    )
    series_total = chans * pulses
    local = echoes.reshape(2, series_total, cells_dev)
    cells = train_cells(gates, TRAIN)
    series_all = lax.all_to_all(local, "range", split_axis=1, concat_axis=2, tiled=True)
    values = series_all.astype(jnp.float32)
    count = values.shape[1]
    padded = jnp.pad(values, ((0, 0), (0, 0), (newlen, nseg * newlen - range_len)))
    blocks = padded.reshape(2, count, nseg + 1, newlen)
    frames = jnp.concatenate([blocks[:, :, :-1], blocks[:, :, 1:]], axis=3).reshape(
        2, count, nseg, radix, radix
    )
    merged = jnp.concatenate([frames[0], frames[1]], axis=-1)
    spectrum = forward_dft(merged, forward_tables)
    shaped = merged_times(spectrum, response)
    outcome = inverse_upper(shaped, inverse_tables)
    out_re = outcome[..., :radix].reshape(count, -1)[:, :range_len] / nfft
    out_im = outcome[..., radix:].reshape(count, -1)[:, :range_len] / nfft
    filtered = jnp.stack([out_re, out_im]).astype(jnp.bfloat16)
    returned = lax.all_to_all(filtered, "range", split_axis=2, concat_axis=1, tiled=True)
    compressed = returned.reshape(2, chans, pulses, cells_dev)
    snapshots = jnp.take(filtered, cells, axis=2)
    partner = partner_2(snapshots, "chan", 0)
    upper = lax.axis_index("chan") == 0
    series_dev = snapshots.shape[1]
    piece = lax.all_gather(snapshots, "range", axis=1, tiled=True)
    joined = jnp.stack([gram(snapshots, piece), gram(partner, piece)], axis=1)
    own_rows = joined[:, 0]
    cross_rows = joined[:, 1]
    other_rows = partner_2(as_sent(cross_rows), "chan", 0).astype(cross_rows.dtype)
    rows_out = jnp.where(
        upper,
        jnp.concatenate([own_rows, other_rows], axis=2),
        jnp.concatenate([other_rows, own_rows], axis=2),
    )
    covariance = (rows_out / TRAIN).reshape(2, 1, series_dev, -1)
    return (compressed, covariance)


def solution(mesh):
    placed = (P("groups", "chan", None, "range"), P(), P("groups", None))
    return jax.shard_map(
        on_device,
        mesh=mesh,
        in_specs=placed,
        out_specs=(P("groups", "chan", None, "range"), P("groups", "chan", "range", None)),
        check_vma=False,
    )
```

profile of v0, /device:TPU:1, one launch (start us, length us, event | category | flops | bytes accessed | tf_op | source)
XLA Modules:
  0.0 279.0 jit_solution(12653052795058454825)
XLA Ops:
  7.2 3.8 %copy.130 = bf16[2,256,8,128]{3,0,2,1:T(2,128)(2,1)} copy(bf16[2,256,8,128]{3,2,1,0:T(8,128)(2,1)} %param.3) | data formatting | bytes 2097152 | tf_op args[0]
  11.0 6.4 %all-to-all-start = ((bf16[2,2048,128]{2,0,1:T(2,128)(2,1)}), bf16[2,2048,128]{2,0,1:T(2,128)(2,1)S(1)}, u32[]{:S(2)}, u32[]{:S(2)}) async-start(bf16[2,2048,128]{2,0,1:T(2,128)(2,1)} %bitcast), calls=%async_computation | async-start | bytes 2097152 | tf_op jit(solution)/shard_map/all_to_all | solution.py:125
  19.5 0.4 fusion.60
  20.1 0.3 fusion.40
  20.8 21.2 %all-to-all-done = bf16[2,2048,128]{2,0,1:T(2,128)(2,1)S(1)} async-done(((bf16[2,2048,128]{2,0,1:T(2,128)(2,1)}), bf16[2,2048,128]{2,0,1:T(2,128)(2,1)S(1)}, u32[]{:S(2)}, u32[]{:S(2)}) %all-to-all-start) | async-done | bytes 1048608 | tf_op jit(solution)/shard_map/all_to_all | solution.py:125
  42.1 0.7 copy.132
  43.1 0.7 fusion.95
  43.8 3.7 %fusion.12 = (f32[1,256,1,4096]{1,3,2,0:T(8,128)}, f32[1,256,1,4096]{1,3,2,0:T(8,128)}) fusion(f32[2,256,1,2048]{1,3,2,0:T(8,128)S(1)} %get-tuple-element.26, f32[2,256,1,2048]{1,3,2,0:T(8,128)S(1)} %get-tuple-element.27), kind=kLoop, calls=%fused_computation.26 | loop fusion | flops 2097152 | bytes 16777216 | tf_op jit(solution)/shard_map/concatenate | solution.py:130
  47.5 9.1 %copy.133 = f32[256,1,64,64]{3,2,0,1:T(8,128)} copy(f32[256,1,64,64]{0,3,2,1:T(8,128)} %bitcast.180) | data formatting | bytes 8388608 | tf_op jit(solution)/shard_map/squeeze | solution.py:133
  56.7 9.1 %copy.134 = f32[256,1,64,64]{3,2,0,1:T(8,128)} copy(f32[256,1,64,64]{0,3,2,1:T(8,128)} %bitcast.179) | data formatting | bytes 8388608 | tf_op jit(solution)/shard_map/squeeze | solution.py:133
  65.8 20.8 %convolution_bitcast_fusion = f32[256,1,2,64,128]{4,3,2,0,1:T(8,128)} fusion(f32[256,1,64,64]{3,2,0,1:T(8,128)} %copy.134, f32[256,1,64,64]{3,2,0,1:T(8,128)} %copy.133, f32[1,64,64]{2,1,0:T(8,128)S(1)} %get-tuple-element.38, f32[1,64,64]{2,1,0:T(8,128)S(1)} %get-tuple-element.39), kind=kOutput, calls=%fused_computation.1 | convolution fusion | flops 3223330816 | bytes 25198592 | tf_op jit(solution)/shard_map/ckn,...nr->...ckr/dot_general | solution.py:68
  86.6 19.7 %multiply_subtract_fusion = (f32[256,1,64,64]{3,2,0,1:T(8,128)}, f32[256,1,64,64]{3,2,0,1:T(8,128)}) fusion(f32[64,64]{1,0:T(8,128)S(1)} %copy.138, f32[64,64]{1,0:T(8,128)S(1)} %copy.137, f32[256,1,2,64,128]{4,3,2,0,1:T(8,128)} %convolution_bitcast_fusion), kind=kLoop, calls=%fused_computation.25 | loop fusion | flops 8388608 | bytes 25198592 | tf_op jit(solution)/shard_map/sub | solution.py:62
  106.3 11.9 %maximum_bitcast_fusion.2 = f32[256,64,128]{2,1,0:T(8,128)} fusion(f32[256,1,64,64]{3,2,0,1:T(8,128)} %get-tuple-element.17, f32[256,1,64,64]{3,2,0,1:T(8,128)} %get-tuple-element.16), kind=kLoop, calls=%fused_computation.13 | loop fusion | flops 2097152 | bytes 16777216 | tf_op jit(solution)/shard_map/reshape.22
  118.2 16.0 %fusion.13 = f32[256,1,64,128]{0,3,2,1:T(8,128)S(1)} fusion(f32[256,64,128]{2,1,0:T(8,128)} %maximum_bitcast_fusion.2, f32[64,64]{0,1:T(8,128)S(1)} %get-tuple-element.41, f32[64,64]{0,1:T(8,128)S(1)} %fusion.84, f32[64,64]{0,1:T(8,128)S(1)} %get-tuple-element.40), kind=kOutput, calls=%fused_computation.35 | convolution fusion | flops 3221274624 | bytes 16826368 | tf_op jit(solution)/shard_map/...km,mj->...kj/dot_general | solution.py:76
  134.2 1.9 multiply_subtract_fusion.2
  136.1 8.5 %fusion.16 = f32[256,1,64,128]{0,3,2,1:T(8,128)S(1)} fusion(f32[256,1,64,64]{0,3,2,1:T(8,128)S(1)} %get-tuple-element.21, f32[256,1,64,64]{0,3,2,1:T(8,128)S(1)} %get-tuple-element.20, f32[64,64]{0,1:T(8,128)S(1)} %get-tuple-element.43, f32[64,64]{0,1:T(8,128)S(1)} %fusion.85, f32[64,64]{0,1:T(8,128)S(1)} %get-tuple-element.42), kind=kOutput, calls=%fused_computation.37 | convolution fusion | flops 3223371776 | bytes 16826368 | tf_op jit(solution)/shard_map/...km,mj->...kj/dot_general | solution.py:76
  144.6 1.5 multiply_subtract_fusion.1
  146.1 4.0 %maximum_bitcast_fusion.5 = f32[256,64,128,1]{0,2,1,3:T(8,128)} fusion(f32[256,1,64,64]{0,3,2,1:T(8,128)S(1)} %get-tuple-element.19, f32[256,1,64,64]{0,3,2,1:T(8,128)S(1)} %get-tuple-element.18), kind=kLoop, calls=%fused_computation.18 | loop fusion | flops 2097152 | bytes 16777216 | tf_op jit(solution)/shard_map/reshape.38
  150.1 8.7 %copy.165 = f32[256,64,128,1]{2,1,3,0:T(8,128)} copy(f32[256,64,128,1]{0,2,1,3:T(8,128)} %maximum_bitcast_fusion.5) | data formatting | bytes 16777216 | tf_op jit(solution)/shard_map/reshape.38
  158.8 12.3 %convolution_bitcast_fusion.1 = f32[256,1,2,32,128]{4,3,2,0,1:T(8,128)} fusion(f32[256,64,128,1]{2,1,3,0:T(8,128)} %copy.165, f32[1,64,64]{2,1,0:T(8,128)S(1)} %get-tuple-element.44, f32[1,64,64]{2,1,0:T(8,128)S(1)} %get-tuple-element.45), kind=kOutput, calls=%fused_computation.36 | convolution fusion | flops 1610616832 | bytes 16809984 | tf_op jit(solution)/shard_map/ckn,...nr->...ckr/dot_general | solution.py:68
  171.2 11.4 %slice_subtract_fusion = (f32[256,1,1,32,64]{4,3,2,0,1:T(8,128)}, f32[256,1,1,32,64]{4,3,2,0,1:T(8,128)}) fusion(f32[256,1,2,32,128]{4,3,2,0,1:T(8,128)} %convolution_bitcast_fusion.1), kind=kLoop, calls=%fused_computation.28 | loop fusion | flops 1048576 | bytes 12582912 | tf_op jit(solution)/shard_map/sub | solution.py:70
  182.5 3.5 %copy.148 = f32[256,1,1,32,64]{0,4,3,2,1:T(8,128)S(1)} copy(f32[256,1,1,32,64]{4,3,2,0,1:T(8,128)} %get-tuple-element.22) | data formatting | bytes 4194304 | tf_op jit(solution)/shard_map/sub | solution.py:70
  186.2 0.8 copy.152
  187.0 3.6 %copy.150 = f32[256,1,1,32,64]{0,4,3,2,1:T(8,128)S(1)} copy(f32[256,1,1,32,64]{4,3,2,0,1:T(8,128)} %get-tuple-element.23) | data formatting | bytes 4194304 | tf_op jit(solution)/shard_map/add | solution.py:71
  190.6 0.8 copy.153
  191.5 3.4 %pad_maximum_fusion.2 = bf16[2,256,1024]{1,0,2:T(2,128)(2,1)} fusion(bf16[1,256,1024]{1,0,2:T(2,128)(2,1)S(1)} %copy.153, bf16[1,256,1024]{1,0,2:T(2,128)(2,1)S(1)} %copy.152), kind=kLoop, calls=%fused_computation.54 | loop fusion | flops 2097152 | bytes 2097152 | tf_op jit(solution)/shard_map/stack | solution.py:139
  194.9 2.1 gather_fusion
  197.0 0.9 fusion.39
  197.9 2.2 collective-permute-start
  200.1 4.2 %all-to-all-start.1 = ((bf16[2,256,1024]{1,0,2:T(2,128)(2,1)}), bf16[2,256,1024]{1,0,2:T(2,128)(2,1)}, u32[]{:S(2)}, u32[]{:S(2)}) async-start(bf16[2,256,1024]{1,0,2:T(2,128)(2,1)} %pad_maximum_fusion.2), calls=%async_computation.1 | async-start | bytes 2097152 | tf_op jit(solution)/shard_map/all_to_all | solution.py:140
  204.8 43.3 %all-gather.2.cloned.1.call-done = bf16[2,2048,128]{1,0,2:T(2,128)(2,1)} async-done(((bf16[2,256,128]{1,0,2:T(2,128)(2,1)}), bf16[2,2048,128]{1,0,2:T(2,128)(2,1)}) %all-gather.2.cloned.1.call-update) | async-done | bytes 1048592 | tf_op jit(solution)/shard_map/all_gather | solution.py:146
  248.1 4.2 %fusion.96 = (bf16[1,2048,128]{1,0,2:T(2,128)(2,1)}, bf16[1,2048,128]{1,0,2:T(2,128)(2,1)S(1)}) fusion(bf16[2,2048,128]{1,0,2:T(2,128)(2,1)} %all-gather.2.cloned.1.call-done), kind=kLoop, calls=%fused_computation.165 | loop fusion | bytes 2097152 | tf_op jit(solution)/shard_map/slice | solution.py:100
  252.3 0.8 copy.158
  253.1 0.4 fusion.29
  253.6 2.4 copy.156
  256.0 0.4 fusion.22
  256.4 0.4 fusion.27
  256.9 0.4 fusion.21
  257.3 1.5 pad_maximum_fusion.1
  258.8 2.2 collective-permute-start.1
  261.5 3.6 %copy.154 = bf16[2,8,256,128]{3,2,1,0:T(8,128)(2,1)} copy(bf16[2,8,256,128]{2,0,3,1:T(2,128)(2,1)} %bitcast.37) | data formatting | bytes 2097152 | tf_op jit(solution)/shard_map/all_to_all | solution.py:140
  265.2 0.4 fusion.37
  265.6 0.4 fusion.18
  266.0 0.4 fusion.35
  266.5 0.4 fusion.17
  266.9 0.5 maximum_bitcast_fusion.6
  267.4 0.5 bitcast_convert_fusion
  268.0 4.0 %fusion.9 = f32[2,1,256,4096]{3,2,1,0:T(8,128)} fusion(f32[2,1,256,2048]{3,2,0,1:T(8,128)S(1)} %bitcast_convert_fusion, f32[2,1,256,2048]{3,2,0,1:T(8,128)S(1)} %maximum_bitcast_fusion.6, pred[]{:T(512)S(6)} %eq.19), kind=kLoop, calls=%fused_computation.21 | loop fusion | flops 8388608 | bytes 16777216
  (48 shorter events, 4.1 us)
Async XLA Ops:
  7.2 10.9 %copy-start.1 = (f32[2,2049]{1,0:T(2,128)S(1)}, f32[2,2049]{1,0:T(2,128)}, u32[]{:S(2)}) copy-start(f32[2,2049]{1,0:T(2,128)} %param.4) | copy-start | bytes 49180
  7.2 11.3 %copy-start.2 = (s32[2,8]{1,0:T(2,128)S(1)}, s32[2,8]{1,0:T(2,128)}, u32[]{:S(2)}) copy-start(s32[2,8]{1,0:T(2,128)} %param.5) | copy-start | bytes 196
  11.0 31.0 %all-to-all-start = ((bf16[2,2048,128]{2,0,1:T(2,128)(2,1)}), bf16[2,2048,128]{2,0,1:T(2,128)(2,1)S(1)}, u32[]{:S(2)}, u32[]{:S(2)}) async-start(bf16[2,2048,128]{2,0,1:T(2,128)(2,1)} %bitcast), calls=%async_computation | async-start | bytes 2097152 | tf_op jit(solution)/shard_map/all_to_all | solution.py:125
  17.4 230.7 %all-gather.2.cloned.1.call-start = ((), (), s32[]{:S(2)}) async-start(), calls=%async_computation.2 | async-start | bytes 1179648 | tf_op jit(solution)/shard_map/all_gather | solution.py:146
  197.9 6.4 %collective-permute-start = (bf16[2,256,128]{1,0,2:T(2,128)(2,1)}, bf16[2,256,128]{1,0,2:T(2,128)(2,1)S(1)}, u32[]{:S(2)}, u32[]{:S(2)}) collective-permute-start(bf16[2,256,128]{1,0,2:T(2,128)(2,1)} %fusion.39), channel_id=1, source_target_pairs={{0,1},{1,0},{2,3},{3,2},{4,5},{5,4},{6,7},{7,6},{8,9},{9,8},{10,11... | collective-permute-start | bytes 393224 | tf_op jit(solution)/shard_map/ppermute | solution.py:14
  200.1 61.4 %all-to-all-start.1 = ((bf16[2,256,1024]{1,0,2:T(2,128)(2,1)}), bf16[2,256,1024]{1,0,2:T(2,128)(2,1)}, u32[]{:S(2)}, u32[]{:S(2)}) async-start(bf16[2,256,1024]{1,0,2:T(2,128)(2,1)} %pad_maximum_fusion.2), calls=%async_computation.1 | async-start | bytes 2097152 | tf_op jit(solution)/shard_map/all_to_all | solution.py:140
  256.9 4.2 %copy-start = (bf16[2,256,128]{1,0,2:T(2,128)(2,1)S(1)}, bf16[2,256,128]{1,0,2:T(2,128)(2,1)}, u32[]{:S(2)}) copy-start(bf16[2,256,128]{1,0,2:T(2,128)(2,1)} %fusion.39) | copy-start | bytes 393220
  258.8 8.6 %collective-permute-start.1 = (bf16[2,256,2048]{2,1,0:T(8,128)(2,1)}, bf16[2,256,2048]{2,1,0:T(8,128)(2,1)S(1)}, u32[]{:S(2)}, u32[]{:S(2)}) collective-permute-start(bf16[2,256,2048]{2,1,0:T(8,128)(2,1)} %pad_maximum_fusion.1), channel_id=1, source_target_pairs={{0,1},{1,0},{2,3},{3,2},{4,5},{5,4},{6,7},{7,6},{8,9},{9,8},{10,11... | collective-permute-start | bytes 6291464 | tf_op jit(solution)/shard_map/ppermute | solution.py:14
Sparse Core Ops, SparseCore 0:
  198.0 50.0 all-gather.1
where the time goes:
time: 284 us; the launch traced here: 279 us
  other arithmetic  66.9 us (24%)
  waiting for transfers between devices  64.5 us (23%)
  matrix products  61.9 us (22%)
  local copies, waits for them, and re-layouts  56 us (20%)
  starting transfers between devices  15 us (5%)
  between operations  14.6 us (5%)
    all_gather x1, waiting for transfers between devices, on_device(): piece = lax.all_gather(snapshots, 'range', axis=1, tiled=True)  43.3 us
    dot_general x3, matrix products, left_section(): jnp.einsum('ckn,...nr->...ckr', stacked, values, precision=lax.Precision....  33.6 us
    dot_general x3, matrix products, right_section(): jnp.einsum('...km,mj->...kj', values, block, precision=lax.Precision.HIGH...  24.8 us
    sub x4, other arithmetic, merged_times(): first_re * second_re - first_im * second_im  23.2 us
    all_to_all x1, waiting for transfers between devices, on_device(): lax.all_to_all(local, 'range', split_axis=1, concat_axis=2, tiled=True)  21.2 us
    squeeze x2, local copies, waits for them, and re-layouts, on_device(): merged = jnp.concatenate([frames[0], frames[1]], axis=-1)  18.2 us
    another operation x3, other arithmetic  16.1 us
    sub x1, other arithmetic, left_section(): real_part = mixed[..., 0, :, :half] - mixed[..., 1, :, half:]  11.4 us
  transfers between devices with their start and end apart: 5, of which 2 were waited for; matrix products, arithmetic and copies ran while one was open for 7% of the time, Pallas kernels for 0%

commit v1 on v0

--- a/solution.py
+++ b/solution.py
@@ -137,7 +137,19 @@
     out_re = outcome[..., :radix].reshape(count, -1)[:, :range_len] / nfft
     out_im = outcome[..., radix:].reshape(count, -1)[:, :range_len] / nfft
     filtered = jnp.stack([out_re, out_im]).astype(jnp.bfloat16)
-    returned = lax.all_to_all(filtered, "range", split_axis=2, concat_axis=1, tiled=True)
+    front = lax.psum(1, "range")
+    step_out, left_arr = (front, lax.axis_index("range"))
+    f_next = filtered.shape[2] // step_out
+    p_next = jnp.roll(filtered, -left_arr * f_next, axis=2)
+    crops = [lax.slice_in_dim(p_next, 0, f_next, axis=2)]
+    for t in range(1, step_out):
+        side_arr = lax.slice_in_dim(p_next, t * f_next, (t + 1) * f_next, axis=2)
+        y_new = lax.ppermute(
+            side_arr, "range", [(dd, (dd + t) % step_out) for dd in range(step_out)]
+        )
+        crops.append(y_new)
+    newest = jnp.concatenate(crops[::-1], axis=1)
+    returned = jnp.roll(newest, (left_arr + 1) * crops[0].shape[1], axis=1)
     compressed = returned.reshape(2, chans, pulses, cells_dev)
     snapshots = jnp.take(filtered, cells, axis=2)
     partner = partner_2(snapshots, "chan", 0)

time: 284 us -> 294 us (1.035)
  local copies, waits for them, and re-layouts: 56 us -> 69.1 us
  waiting for transfers between devices: 64.5 us -> 52.9 us
  other arithmetic: 66.9 us -> 75.4 us
    all_gather x1, waiting for transfers between devices: 43.3 us -> 15.4 us  [on_device(): piece = lax.all_gather(snapshots, 'range', axis=1, tiled=True)]
    ppermute x0 -> x7, waiting for transfers between devices: none -> 16.4 us  [on_device(): lax.ppermute(side_arr, 'range', [(dd, (dd + t) % step_out) for dd in rang...]
    unnamed x7 -> x28, local copies, waits for them, and re-layouts: 3.85 us -> 15.1 us
    another operation x3, other arithmetic: 3.57 us -> 10.5 us  [on_device(): filtered = jnp.stack([out_re, out_im]).astype(jnp.bfloat16)]
    ppermute x0 -> x7, starting transfers between devices: none -> 6.01 us  [on_device(): lax.ppermute(side_arr, 'range', [(dd, (dd + t) % step_out) for dd in rang...]
    all_to_all x1 -> x0, starting transfers between devices: 4.24 us -> none  [on_device(): lax.all_to_all(filtered, 'range', split_axis=2, concat_axis=1, tiled=True)]
    dynamic_slice x0 -> x2, local copies, waits for them, and re-layouts: none -> 4.04 us  [on_device(): returned = jnp.roll(newest, (left_arr + 1) * crops[0].shape[1], axis=1)]
    all_to_all x1 -> x0, local copies, waits for them, and re-layouts: 3.64 us -> none  [on_device(): lax.all_to_all(filtered, 'range', split_axis=2, concat_axis=1, tiled=True)]
  transfers between devices with their start and end apart: 5 -> 11, of which waited for: 2 -> 6; matrix products, arithmetic and copies ran while one was open for 7% -> 8% of each run, Pallas kernels for 0% -> 0%
where the time goes in v1:
time: 294 us; the launch traced here: 289 us
  other arithmetic  75.4 us (26%)
  local copies, waits for them, and re-layouts  69.1 us (24%)
  matrix products  61.9 us (21%)
  waiting for transfers between devices  52.9 us (18%)
  starting transfers between devices  15.1 us (5%)
  between operations  15 us (5%)
    dot_general x3, matrix products, left_section(): jnp.einsum('ckn,...nr->...ckr', stacked, values, precision=lax.Precision....  33.6 us
    dot_general x3, matrix products, right_section(): jnp.einsum('...km,mj->...kj', values, block, precision=lax.Precision.HIGH...  24.8 us
    sub x4, other arithmetic, merged_times(): first_re * second_re - first_im * second_im  23.1 us
    all_to_all x1, waiting for transfers between devices, on_device(): lax.all_to_all(local, 'range', split_axis=1, concat_axis=2, tiled=True)  21.2 us
    squeeze x2, local copies, waits for them, and re-layouts, on_device(): merged = jnp.concatenate([frames[0], frames[1]], axis=-1)  18.3 us
    ppermute x7, waiting for transfers between devices, on_device(): lax.ppermute(side_arr, 'range', [(dd, (dd + t) % step_out) for dd in rang...  16.4 us
    another operation x3, other arithmetic  16.1 us
    all_gather x1, waiting for transfers between devices, on_device(): piece = lax.all_gather(snapshots, 'range', axis=1, tiled=True)  15.4 us
  transfers between devices with their start and end apart: 11, of which 6 were waited for; matrix products, arithmetic and copies ran while one was open for 8% of the time, Pallas kernels for 0%

profile of v1, /device:TPU:1, one launch (start us, length us, event | category | flops | bytes accessed | tf_op | source)
XLA Modules:
  0.0 289.5 jit_solution(10814845574702148751)
XLA Ops:
  7.2 3.8 %copy.128 = bf16[2,256,8,128]{3,0,2,1:T(2,128)(2,1)} copy(bf16[2,256,8,128]{3,2,1,0:T(8,128)(2,1)} %param.3) | data formatting | bytes 2097152 | tf_op args[0]
  11.0 6.4 %all-to-all-start = ((bf16[2,2048,128]{2,0,1:T(2,128)(2,1)}), bf16[2,2048,128]{2,0,1:T(2,128)(2,1)S(1)}, u32[]{:S(2)}, u32[]{:S(2)}) async-start(bf16[2,2048,128]{2,0,1:T(2,128)(2,1)} %bitcast), calls=%async_computation | async-start | bytes 2097152 | tf_op jit(solution)/shard_map/all_to_all | solution.py:125
  20.8 21.2 %all-to-all-done = bf16[2,2048,128]{2,0,1:T(2,128)(2,1)S(1)} async-done(((bf16[2,2048,128]{2,0,1:T(2,128)(2,1)}), bf16[2,2048,128]{2,0,1:T(2,128)(2,1)S(1)}, u32[]{:S(2)}, u32[]{:S(2)}) %all-to-all-start) | async-done | bytes 1048608 | tf_op jit(solution)/shard_map/all_to_all | solution.py:125
  43.9 3.7 %fusion.12 = (f32[1,256,1,4096]{1,3,2,0:T(8,128)}, f32[1,256,1,4096]{1,3,2,0:T(8,128)}) fusion(f32[2,256,1,2048]{1,3,2,0:T(8,128)S(1)} %get-tuple-element.26, f32[2,256,1,2048]{1,3,2,0:T(8,128)S(1)} %get-tuple-element.27), kind=kLoop, calls=%fused_computation.26 | loop fusion | flops 2097152 | bytes 16777216 | tf_op jit(solution)/shard_map/concatenate | solution.py:130
  47.6 9.2 %copy.131 = f32[256,1,64,64]{3,2,0,1:T(8,128)} copy(f32[256,1,64,64]{0,3,2,1:T(8,128)} %bitcast.177) | data formatting | bytes 8388608 | tf_op jit(solution)/shard_map/squeeze | solution.py:133
  56.7 9.1 %copy.132 = f32[256,1,64,64]{3,2,0,1:T(8,128)} copy(f32[256,1,64,64]{0,3,2,1:T(8,128)} %bitcast.176) | data formatting | bytes 8388608 | tf_op jit(solution)/shard_map/squeeze | solution.py:133
  65.8 20.8 %convolution_bitcast_fusion = f32[256,1,2,64,128]{4,3,2,0,1:T(8,128)} fusion(f32[256,1,64,64]{3,2,0,1:T(8,128)} %copy.132, f32[256,1,64,64]{3,2,0,1:T(8,128)} %copy.131, f32[1,64,64]{2,1,0:T(8,128)S(1)} %get-tuple-element.47, f32[1,64,64]{2,1,0:T(8,128)S(1)} %get-tuple-element.48), kind=kOutput, calls=%fused_computation.1 | convolution fusion | flops 3223330816 | bytes 25198592 | tf_op jit(solution)/shard_map/ckn,...nr->...ckr/dot_general | solution.py:68
  86.6 19.9 %multiply_subtract_fusion = (f32[256,1,64,64]{3,2,0,1:T(8,128)}, f32[256,1,64,64]{3,2,0,1:T(8,128)}) fusion(f32[64,64]{1,0:T(8,128)S(1)} %copy.136, f32[64,64]{1,0:T(8,128)S(1)} %copy.135, f32[256,1,2,64,128]{4,3,2,0,1:T(8,128)} %convolution_bitcast_fusion), kind=kLoop, calls=%fused_computation.25 | loop fusion | flops 8388608 | bytes 25198592 | tf_op jit(solution)/shard_map/sub | solution.py:62
  106.5 11.9 %maximum_bitcast_fusion.2 = f32[256,64,128]{2,1,0:T(8,128)} fusion(f32[256,1,64,64]{3,2,0,1:T(8,128)} %get-tuple-element.17, f32[256,1,64,64]{3,2,0,1:T(8,128)} %get-tuple-element.16), kind=kLoop, calls=%fused_computation.13 | loop fusion | flops 2097152 | bytes 16777216 | tf_op jit(solution)/shard_map/reshape.22
  118.5 16.0 %fusion.13 = f32[256,1,64,128]{0,3,2,1:T(8,128)S(1)} fusion(f32[256,64,128]{2,1,0:T(8,128)} %maximum_bitcast_fusion.2, f32[64,64]{0,1:T(8,128)S(1)} %get-tuple-element.50, f32[64,64]{0,1:T(8,128)S(1)} %fusion.87, f32[64,64]{0,1:T(8,128)S(1)} %get-tuple-element.49), kind=kOutput, calls=%fused_computation.35 | convolution fusion | flops 3221274624 | bytes 16826368 | tf_op jit(solution)/shard_map/...km,mj->...kj/dot_general | solution.py:76
  134.5 1.6 multiply_subtract_fusion.2
  136.1 8.5 %fusion.16 = f32[256,1,64,128]{0,3,2,1:T(8,128)S(1)} fusion(f32[256,1,64,64]{0,3,2,1:T(8,128)S(1)} %get-tuple-element.21, f32[256,1,64,64]{0,3,2,1:T(8,128)S(1)} %get-tuple-element.20, f32[64,64]{0,1:T(8,128)S(1)} %get-tuple-element.52, f32[64,64]{0,1:T(8,128)S(1)} %fusion.88, f32[64,64]{0,1:T(8,128)S(1)} %get-tuple-element.51), kind=kOutput, calls=%fused_computation.37 | convolution fusion | flops 3223371776 | bytes 16826368 | tf_op jit(solution)/shard_map/...km,mj->...kj/dot_general | solution.py:76
  144.6 1.5 multiply_subtract_fusion.1
  146.1 4.0 %maximum_bitcast_fusion.5 = f32[256,64,128,1]{0,2,1,3:T(8,128)} fusion(f32[256,1,64,64]{0,3,2,1:T(8,128)S(1)} %get-tuple-element.19, f32[256,1,64,64]{0,3,2,1:T(8,128)S(1)} %get-tuple-element.18), kind=kLoop, calls=%fused_computation.18 | loop fusion | flops 2097152 | bytes 16777216 | tf_op jit(solution)/shard_map/reshape.38
  150.1 8.7 %copy.163 = f32[256,64,128,1]{2,1,3,0:T(8,128)} copy(f32[256,64,128,1]{0,2,1,3:T(8,128)} %maximum_bitcast_fusion.5) | data formatting | bytes 16777216 | tf_op jit(solution)/shard_map/reshape.38
  158.8 12.4 %convolution_bitcast_fusion.1 = f32[256,1,2,32,128]{4,3,2,0,1:T(8,128)} fusion(f32[256,64,128,1]{2,1,3,0:T(8,128)} %copy.163, f32[1,64,64]{2,1,0:T(8,128)S(1)} %get-tuple-element.53, f32[1,64,64]{2,1,0:T(8,128)S(1)} %get-tuple-element.54), kind=kOutput, calls=%fused_computation.36 | convolution fusion | flops 1610616832 | bytes 16809984 | tf_op jit(solution)/shard_map/ckn,...nr->...ckr/dot_general | solution.py:68
  171.2 11.4 %slice_subtract_fusion = (f32[256,1,1,32,64]{4,3,2,0,1:T(8,128)}, f32[256,1,1,32,64]{4,3,2,0,1:T(8,128)}) fusion(f32[256,1,2,32,128]{4,3,2,0,1:T(8,128)} %convolution_bitcast_fusion.1), kind=kLoop, calls=%fused_computation.28 | loop fusion | flops 1048576 | bytes 12582912 | tf_op jit(solution)/shard_map/sub | solution.py:70
  182.6 3.5 %copy.146 = f32[256,1,1,32,64]{0,4,3,2,1:T(8,128)S(1)} copy(f32[256,1,1,32,64]{4,3,2,0,1:T(8,128)} %get-tuple-element.22) | data formatting | bytes 4194304 | tf_op jit(solution)/shard_map/sub | solution.py:70
  186.3 0.8 copy.150
  187.1 3.6 %copy.148 = f32[256,1,1,32,64]{0,4,3,2,1:T(8,128)S(1)} copy(f32[256,1,1,32,64]{4,3,2,0,1:T(8,128)} %get-tuple-element.23) | data formatting | bytes 4194304 | tf_op jit(solution)/shard_map/add | solution.py:71
  190.7 0.8 copy.151
  191.5 10.3 %pad_maximum_fusion.2 = (bf16[2,256,1024]{1,0,2:T(2,128)(2,1)S(1)}, bf16[2,256,1024]{1,0,2:T(2,128)(2,1)S(1)}) fusion(bf16[1,256,1024]{1,0,2:T(2,128)(2,1)S(1)} %copy.151, bf16[1,256,1024]{1,0,2:T(2,128)(2,1)S(1)} %copy.150, s32[]{:T(128)S(6)} %select_n.114), kind=kLoop, calls=%fused_computation.60 | loop fusion | flops 6291456 | bytes 3145732 | tf_op jit(solution)/shard_map/stack | solution.py:139
  201.9 0.9 gather_fusion
  202.8 0.9 fusion.42
  203.7 2.2 collective-permute-start.7
  206.5 1.2 fusion.101
  208.0 2.1 collective-permute-start
  210.1 2.4 collective-permute-start.3
  212.5 1.4 collective-permute-start.4
  214.2 0.7 constant_dynamic-update-slice_fusion.13
  215.0 2.8 collective-permute-done.1
  217.8 0.7 constant_dynamic-update-slice_fusion.12
  219.4 12.4 %collective-permute-done.3 = bf16[2,256,128]{1,0,2:T(2,128)(2,1)S(1)} collective-permute-done((bf16[2,256,128]{1,0,2:T(2,128)(2,1)S(1)}, bf16[2,256,128]{1,0,2:T(2,128)(2,1)S(1)}, u32[]{:S(2)}, u32[]{:S(2)}) %collective-permute-start.3) | collective-permute-done | bytes 131104 | tf_op jit(solution)/shard_map/ppermute | solution.py:147
  231.8 0.7 constant_dynamic-update-slice_fusion.10
  232.6 1.0 collective-permute-done.4
  234.6 0.8 constant_dynamic-update-slice_fusion.8
  235.3 0.7 constant_dynamic-update-slice_fusion.7
  239.8 15.4 %all-gather.2.cloned.1.call-done = bf16[2,2048,128]{1,0,2:T(2,128)(2,1)} async-done(((bf16[2,256,128]{1,0,2:T(2,128)(2,1)}), bf16[2,2048,128]{1,0,2:T(2,128)(2,1)}) %all-gather.2.cloned.1.call-update) | async-done | bytes 1048592 | tf_op jit(solution)/shard_map/all_gather | solution.py:158
  255.2 4.5 %fusion.99 = (bf16[1,2048,128]{1,0,2:T(2,128)(2,1)}, bf16[1,2048,128]{1,0,2:T(2,128)(2,1)S(1)}) fusion(bf16[2,2048,128]{1,0,2:T(2,128)(2,1)} %all-gather.2.cloned.1.call-done), kind=kLoop, calls=%fused_computation.189 | loop fusion | bytes 2097152 | tf_op jit(solution)/shard_map/slice | solution.py:100
  259.7 2.4 copy.154
  262.1 0.9 copy.156
  264.7 1.5 pad_maximum_fusion.1
  267.5 0.7 constant_dynamic-update-slice_fusion.1
  268.2 0.7 constant_dynamic-update-slice_fusion
  269.7 1.9 constant_dynamic-slice_fusion
  271.7 2.1 copy.152
  276.0 2.1 bitcast_convert_fusion
  278.1 4.0 %fusion.9 = f32[2,1,256,4096]{3,2,1,0:T(8,128)} fusion(f32[2,1,256,2048]{3,2,0,1:T(8,128)S(1)} %bitcast_convert_fusion, f32[2,1,256,2048]{3,2,0,1:T(8,128)S(1)} %maximum_bitcast_fusion.6, pred[]{:T(512)S(6)} %eq.24), kind=kLoop, calls=%fused_computation.21 | loop fusion | flops 8388608 | bytes 16777216
  (84 shorter events, 18.2 us)
Async XLA Ops:
  7.2 11.0 %copy-start.4 = (f32[2,2049]{1,0:T(2,128)S(1)}, f32[2,2049]{1,0:T(2,128)}, u32[]{:S(2)}) copy-start(f32[2,2049]{1,0:T(2,128)} %param.4) | copy-start | bytes 49180
  7.2 11.3 %copy-start.5 = (s32[2,8]{1,0:T(2,128)S(1)}, s32[2,8]{1,0:T(2,128)}, u32[]{:S(2)}) copy-start(s32[2,8]{1,0:T(2,128)} %param.5) | copy-start | bytes 196
  11.0 31.0 %all-to-all-start = ((bf16[2,2048,128]{2,0,1:T(2,128)(2,1)}), bf16[2,2048,128]{2,0,1:T(2,128)(2,1)S(1)}, u32[]{:S(2)}, u32[]{:S(2)}) async-start(bf16[2,2048,128]{2,0,1:T(2,128)(2,1)} %bitcast), calls=%async_computation | async-start | bytes 2097152 | tf_op jit(solution)/shard_map/all_to_all | solution.py:125
  17.4 237.8 %all-gather.2.cloned.1.call-start = ((), (), s32[]{:S(2)}) async-start(), calls=%async_computation.1 | async-start | bytes 1179648 | tf_op jit(solution)/shard_map/all_gather | solution.py:158
  203.7 8.8 %collective-permute-start.7 = (bf16[2,256,128]{1,0,2:T(2,128)(2,1)}, bf16[2,256,128]{1,0,2:T(2,128)(2,1)S(1)}, u32[]{:S(2)}, u32[]{:S(2)}) collective-permute-start(bf16[2,256,128]{1,0,2:T(2,128)(2,1)} %fusion.42), channel_id=1, source_target_pairs={{0,1},{1,0},{2,3},{3,2},{4,5},{5,4},{6,7},{7,6},{8,9},{9,8},{10,11... | collective-permute-start | bytes 393224 | tf_op jit(solution)/shard_map/ppermute | solution.py:14
  208.0 6.1 %collective-permute-start = (bf16[2,256,128]{1,0,2:T(2,128)(2,1)S(1)}, bf16[2,256,128]{1,0,2:T(2,128)(2,1)S(1)}, u32[]{:S(2)}, u32[]{:S(2)}) collective-permute-start(bf16[2,256,128]{1,0,2:T(2,128)(2,1)S(1)} %get-tuple-element.38), channel_id=1, source_target_pairs={{0,14},{2,0},{4,2},{6,4},{8,6},{10,8},{12,10},{14,12},{1,15},{3,1}... | collective-permute-start | bytes 393224 | tf_op jit(solution)/shard_map/ppermute | solution.py:147
  210.1 7.7 %collective-permute-start.1 = (bf16[2,256,128]{1,0,2:T(2,128)(2,1)S(1)}, bf16[2,256,128]{1,0,2:T(2,128)(2,1)S(1)}, u32[]{:S(2)}, u32[]{:S(2)}) collective-permute-start(bf16[2,256,128]{1,0,2:T(2,128)(2,1)S(1)} %get-tuple-element.37), channel_id=1, source_target_pairs={{0,12},{2,14},{4,0},{6,2},{8,4},{10,6},{12,8},{14,10},{1,13},{3,15... | collective-permute-start | bytes 393224 | tf_op jit(solution)/shard_map/ppermute | solution.py:147
  210.1 8.6 %collective-permute-start.2 = (bf16[2,256,128]{1,0,2:T(2,128)(2,1)S(1)}, bf16[2,256,128]{1,0,2:T(2,128)(2,1)S(1)}, u32[]{:S(2)}, u32[]{:S(2)}) collective-permute-start(bf16[2,256,128]{1,0,2:T(2,128)(2,1)S(1)} %get-tuple-element.36), channel_id=1, source_target_pairs={{0,10},{2,12},{4,14},{6,0},{8,2},{10,4},{12,6},{14,8},{1,11},{3,13... | collective-permute-start | bytes 393224 | tf_op jit(solution)/shard_map/ppermute | solution.py:147
  210.1 21.7 %collective-permute-start.3 = (bf16[2,256,128]{1,0,2:T(2,128)(2,1)S(1)}, bf16[2,256,128]{1,0,2:T(2,128)(2,1)S(1)}, u32[]{:S(2)}, u32[]{:S(2)}) collective-permute-start(bf16[2,256,128]{1,0,2:T(2,128)(2,1)S(1)} %get-tuple-element.35), channel_id=1, source_target_pairs={{0,8},{2,10},{4,12},{6,14},{8,0},{10,2},{12,4},{14,6},{1,9},{3,11}... | collective-permute-start | bytes 393224 | tf_op jit(solution)/shard_map/ppermute | solution.py:147
  212.5 21.0 %collective-permute-start.4 = (bf16[2,256,128]{1,0,2:T(2,128)(2,1)S(1)}, bf16[2,256,128]{1,0,2:T(2,128)(2,1)S(1)}, u32[]{:S(2)}, u32[]{:S(2)}) collective-permute-start(bf16[2,256,128]{1,0,2:T(2,128)(2,1)S(1)} %get-tuple-element.34), channel_id=1, source_target_pairs={{0,6},{2,8},{4,10},{6,12},{8,14},{10,0},{12,2},{14,4},{1,7},{3,9},... | collective-permute-start | bytes 393224 | tf_op jit(solution)/shard_map/ppermute | solution.py:147
  214.1 20.4 %collective-permute-start.5 = (bf16[2,256,128]{1,0,2:T(2,128)(2,1)S(1)}, bf16[2,256,128]{1,0,2:T(2,128)(2,1)S(1)}, u32[]{:S(2)}, u32[]{:S(2)}) collective-permute-start(bf16[2,256,128]{1,0,2:T(2,128)(2,1)S(1)} %get-tuple-element.33), channel_id=1, source_target_pairs={{0,4},{2,6},{4,8},{6,10},{8,12},{10,14},{12,0},{14,2},{1,5},{3,7},... | collective-permute-start | bytes 393224 | tf_op jit(solution)/shard_map/ppermute | solution.py:147
  217.8 17.6 %collective-permute-start.6 = (bf16[2,256,128]{1,0,2:T(2,128)(2,1)S(1)}, bf16[2,256,128]{1,0,2:T(2,128)(2,1)S(1)}, u32[]{:S(2)}, u32[]{:S(2)}) collective-permute-start(bf16[2,256,128]{1,0,2:T(2,128)(2,1)S(1)} %get-tuple-element.32), channel_id=1, source_target_pairs={{0,2},{2,4},{4,6},{6,8},{8,10},{10,12},{12,14},{14,0},{1,3},{3,5},... | collective-permute-start | bytes 393224 | tf_op jit(solution)/shard_map/ppermute | solution.py:147
  234.6 25.1 %copy-start = (bf16[2,256,128]{1,0,2:T(2,128)(2,1)}, bf16[2,256,128]{1,0,2:T(2,128)(2,1)S(1)}, u32[]{:S(2)}) copy-start(bf16[2,256,128]{1,0,2:T(2,128)(2,1)S(1)} %collective-permute-done.5) | copy-start | bytes 393220
  235.3 24.3 %copy-start.2 = (bf16[2,256,128]{1,0,2:T(2,128)(2,1)}, bf16[2,256,128]{1,0,2:T(2,128)(2,1)S(1)}, u32[]{:S(2)}) copy-start(bf16[2,256,128]{1,0,2:T(2,128)(2,1)S(1)} %collective-permute-done.6) | copy-start | bytes 393220
  264.3 3.2 %copy-start.1 = (bf16[2,256,128]{1,0,2:T(2,128)(2,1)S(1)}, bf16[2,256,128]{1,0,2:T(2,128)(2,1)}, u32[]{:S(2)}) copy-start(bf16[2,256,128]{1,0,2:T(2,128)(2,1)} %copy-done) | copy-start | bytes 393220
  264.3 4.0 %copy-start.3 = (bf16[2,256,128]{1,0,2:T(2,128)(2,1)S(1)}, bf16[2,256,128]{1,0,2:T(2,128)(2,1)}, u32[]{:S(2)}) copy-start(bf16[2,256,128]{1,0,2:T(2,128)(2,1)} %copy-done.2) | copy-start | bytes 393220
  266.2 9.8 %collective-permute-start.8 = (bf16[2,256,2048]{2,1,0:T(8,128)(2,1)}, bf16[2,256,2048]{2,1,0:T(8,128)(2,1)}, u32[]{:S(2)}, u32[]{:S(2)}) collective-permute-start(bf16[2,256,2048]{2,1,0:T(8,128)(2,1)} %pad_maximum_fusion.1), channel_id=1, source_target_pairs={{0,1},{1,0},{2,3},{3,2},{4,5},{5,4},{6,7},{7,6},{8,9},{9,8},{10,11... | collective-permute-start | bytes 6291464 | tf_op jit(solution)/shard_map/ppermute | solution.py:14
Sparse Core Ops, SparseCore 0:
  203.8 51.3 all-gather.1
